TPU v7x, 512 devices: a whole 4x4x16 slice. The times are simulated.
512 devices in a mesh: section: 8 (over z_hi, core), tp: 64 (over x, z_lo, y).
Axes of the slice: x: 4, y: 4, z: 16 (z_hi: 4, z_lo: 4; z = z_hi * 4 + z_lo), core: 2. Of those that a mesh axis runs over, the one named last changes fastest.
Arguments:
- incoming: bfloat16 [8, 320, 8192], P('section', None, 'tp'), may hold values from -6 to 6
- norm_gain: bfloat16 [8, 8192], P('section', 'tp'), may hold values from 0.5 to 1.5
- query_weight: bfloat16 [8, 8192, 8192], P('section', 'tp'), may hold values from -0.0625 to 0.0625
- query_scale: float32 [8, 64, 64], P('section', 'tp'), may hold values from 0.3 to 3
- query_keep: int32 [8, 64, 64], P('section', 'tp'), may hold values from 0 to 1, as said below
- kv_weight: bfloat16 [8, 8192, 2048], P('section', 'tp'), may hold values from -0.0625 to 0.0625
- kv_scale: float32 [8, 64, 16], P('section', 'tp'), may hold values from 0.3 to 3
- kv_keep: int32 [8, 64, 16], P('section', 'tp'), may hold values from 0 to 1, as said below
- out_weight: bfloat16 [8, 8192, 8192], P('section', 'tp'), may hold values from -0.0625 to 0.0625
- out_scale: float32 [8, 64, 64], P('section', 'tp'), may hold values from 0.3 to 3
- out_keep: int32 [8, 64, 64], P('section', 'tp'), may hold values from 0 to 1, as said below
- documents: int32 [320], replicated, may hold values from 0 to 3, never falling along the last dimension, each value on 1 to 160 neighbouring positions
Outputs:
- passed: bfloat16 [8, 320, 8192], P('section', None, 'tp')
Inputs may be any that keep to these rules, and one draw needn't show every extreme that they name: `documents`: document numbers never fall along the tokens; every document has 1 to 160 tokens and one has exactly 160. `query_keep`: 1 keeps the block, 0 removes it. `kv_keep`: 1 keeps the block, 0 removes it. `out_keep`: 1 keeps the block, 0 removes it.
All inputs are finite; a program needn't handle non-finite values.
Results may differ from a plain program's by a relative error of at most 0.006.
Values may be sent and summed in bfloat16 or wider, within the bound.
No kernel may reach another device: no remote copies, remote signals or barrier semaphores. Data moves between devices by JAX's collectives and lax.ppermute only.
A program may use at most 64 MiB of HBM per device.

v0:
```python
import jax
import jax.numpy as jnp
from jax import lax
from jax.sharding import PartitionSpec as P

D = 8192
HEADS = 64
KV_HEADS = 8
HD = 128
BLK = 128
rope_base = 500000.0
epsilon = 1e-05


def passed_along(value, axis, steps):
    count = lax.axis_size(axis)
    pairs = [(source, (source + steps) % count) for source in range(count)]
    return lax.ppermute(value, axis, pairs)


def dequant(weight, scale, keep):
    row_count, col_count = weight.shape
    factor = scale * keep.astype(jnp.float32)
    blocks = weight.astype(jnp.float32).reshape(row_count // BLK, BLK, col_count // BLK, BLK)
    blocks = blocks * factor[:, None, :, None]
    return blocks.reshape(row_count, col_count).astype(jnp.bfloat16)


def rotate(values, first_col):
    row_count, col_count = values.shape
    columns = first_col + 2 * jnp.arange(col_count // 2, dtype=jnp.int32)
    frequency = rope_base ** (-(columns % HD).astype(jnp.float32) / HD)
    angles = jnp.arange(row_count, dtype=jnp.float32)[:, None] * frequency[None, :]
    paired = values.reshape(row_count, col_count // 2, 2)
    even_part = paired[:, :, 0]
    odd_part = paired[:, :, 1]
    cosine = jnp.cos(angles)
    sine = jnp.sin(angles)
    turned = jnp.stack(
        (even_part * cosine - odd_part * sine, even_part * sine + odd_part * cosine), axis=-1
    )
    return turned.reshape(row_count, col_count)


def rotate_keys(values, first_col, kv_width):
    col_ids = first_col + jnp.arange(values.shape[1], dtype=jnp.int32)
    return jnp.where(col_ids[None, :] < kv_width, rotate(values, first_col), values)


def local(
    incoming,
    norm_gain,
    query_weight,
    query_scale,
    query_keep,
    kv_weight,
    kv_scale,
    kv_keep,
    out_weight,
    out_scale,
    out_keep,
    documents,
):
    own_index = lax.axis_index("tp")
    local_rows = incoming[0]
    tok_count, own_width = local_rows.shape
    activ = local_rows.astype(jnp.float32)
    kv_width = KV_HEADS * HD
    group_size = HEADS // KV_HEADS
    partial_value = jnp.sum(activ * activ, axis=1, keepdims=True)
    squares = lax.psum(partial_value, "tp")
    normed = (activ * lax.rsqrt(squares / D + epsilon) * norm_gain[0].astype(jnp.float32)).astype(
        jnp.bfloat16
    )
    normed_all = lax.all_gather(normed, "tp", axis=1, tiled=True)
    q_eff = dequant(query_weight[0], query_scale[0], query_keep[0])
    q_columns = lax.all_to_all(q_eff, "tp", split_axis=1, concat_axis=0, tiled=True)
    q_width = q_columns.shape[1]
    queries = jnp.dot(normed_all, q_columns, preferred_element_type=jnp.float32)
    queries = rotate(queries, own_index * q_width).astype(jnp.bfloat16)
    kv_eff = dequant(kv_weight[0], kv_scale[0], kv_keep[0])
    kv_total = lax.psum(jnp.dot(normed, kv_eff, preferred_element_type=jnp.float32), "tp")
    keyval = rotate_keys(kv_total, 0, kv_width).astype(jnp.bfloat16)
    heads_here = q_width // HD
    kv_index = own_index * heads_here // group_size
    key_rows = lax.dynamic_slice_in_dim(keyval, kv_index * HD, HD, 1)
    value_rows = lax.dynamic_slice_in_dim(keyval, kv_width + kv_index * HD, HD, 1)
    token_ids = jnp.arange(tok_count, dtype=jnp.int32)
    allowed = (documents[:, None] == documents[None, :]) & (
        token_ids[:, None] >= token_ids[None, :]
    )
    query_three = queries.reshape(tok_count, heads_here, HD)
    scores = jnp.einsum(
        "thd,sd->hts", query_three, key_rows, preferred_element_type=jnp.float32
    ) / jnp.sqrt(jnp.float32(HD))
    exp_scores = jnp.where(allowed[None], jnp.exp(scores), jnp.float32(0.0))
    probs = (exp_scores / jnp.sum(exp_scores, axis=-1, keepdims=True)).astype(jnp.bfloat16)
    head_out = jnp.einsum("hts,sd->thd", probs, value_rows, preferred_element_type=jnp.float32)
    head_out = head_out.astype(jnp.bfloat16).reshape(tok_count, q_width)
    o_eff = dequant(out_weight[0], out_scale[0], out_keep[0])
    o_columns = lax.all_to_all(o_eff, "tp", split_axis=1, concat_axis=0, tiled=True)
    mixed_sum = jnp.dot(
        lax.all_gather(head_out, "tp", axis=1, tiled=True),
        o_columns,
        preferred_element_type=jnp.float32,
    )
    layer_out = (activ + mixed_sum).astype(jnp.bfloat16)
    received = passed_along(layer_out, "section", 1)
    return received[None]


def solution(mesh):
    placed = (
        P("section", None, "tp"),
        P("section", "tp"),
        P("section", "tp", None),
        P("section", "tp", None),
        P("section", "tp", None),
        P("section", "tp", None),
        P("section", "tp", None),
        P("section", "tp", None),
        P("section", "tp", None),
        P("section", "tp", None),
        P("section", "tp", None),
        P(),
    )
    return jax.shard_map(
        local, mesh=mesh, in_specs=placed, out_specs=P("section", None, "tp"), check_vma=False
    )
```

profile of v0, /device:TPU:1, one launch (start us, length us, event | category | flops | bytes accessed | tf_op | source)
XLA Modules:
  0.0 1547.2 jit_solution(16440638860779838320)
XLA Ops:
  6.5 1.0 fusion.27
  7.6 163.6 %psum.14 = f32[320,1]{0,1:T(1,128)S(1)} all-reduce(f32[320,1]{0,1:T(1,128)S(1)} %broadcast_in_dim.16), channel_id=1, replica_groups=mesh['section'=8,'tp'=64] {'tp'}, use_global_device_ids=true, to_apply=%region_1.0 | all-reduce | flops 320 | bytes 2560 | tf_op jit(solution)/shard_map/psum | solution.py:71
  171.2 0.7 bitcast_convert_fusion
  171.8 0.7 multiply_bitcast_fusion.2
  172.5 0.1 broadcast_bitcast_fusion
  172.6 3.2 fusion.20
  175.7 0.0 all-reduce.2.cloned.1.call-update
  175.8 0.0 all-gather.4.cloned.1.call-start
  175.8 0.8 copy-done.2
  176.6 0.7 fusion.29
  177.4 0.0 all-gather.4.cloned.1.call-update
  177.4 0.0 copy-start.5
  177.4 3.2 copy.32
  180.7 1.9 fusion.5
  182.5 5.6 all-to-all-start
  188.1 0.0 all-gather.6.cloned.1.call-start
  188.2 699.4 %all-reduce.2.cloned.1.call-done = f32[320,2048]{1,0:T(8,128)} async-done(((f32[320,2048]{1,0:T(8,128)}), f32[320,2048]{1,0:T(8,128)}) %all-reduce.2.cloned.1.call-update) | async-done | bytes 2621456 | tf_op jit(solution)/shard_map/psum | solution.py:82
  887.7 3.5 copy.27
  891.2 3.7 reshape.383
  894.9 4.1 fusion.55
  899.0 3.7 copy.39
  902.7 3.5 copy.40
  906.2 7.1 multiply_subtract_fusion
  913.3 0.1 pad_maximum_fusion
  913.4 2.4 copy.30
  915.8 2.2 reshape.384
  918.0 2.7 copy.31
  920.7 2.8 select_convert_fusion
  923.5 3.2 copy.33
  926.7 2.9 copy.34
  929.6 3.2 dot_general.21
  932.8 255.4 %all-gather.4.cloned.1.call-done = bf16[320,8192]{1,0:T(8,128)(2,1)} async-done(((bf16[320,128]{1,0:T(8,128)(2,1)}), bf16[320,8192]{1,0:T(8,128)(2,1)}) %all-gather.4.cloned.1.call-update) | async-done | bytes 5242896 | tf_op jit(solution)/shard_map/all_gather | solution.py:75
  1188.2 5.1 fusion.2
  1193.3 0.5 subtract_convert_fusion
  1193.8 0.1 copy.36
  1193.9 0.1 convert_element_type.151
  1194.0 1.2 fusion.56
  1195.2 1.8 fusion.18
  1197.0 0.0 all-gather.6.cloned.1.call-update
  1197.0 3.4 copy.37
  1200.5 0.5 fusion.4
  1201.0 37.8 %all_to_all.32 = bf16[128,64,128]{0,2,1:T(8,128)(2,1)S(1)} all-to-all(bf16[128,64,128]{0,2,1:T(8,128)(2,1)S(1)} %fusion.4), channel_id=1, replica_groups=mesh['section'=8,'tp'=64] {'tp'}, dimensions={1} | all-to-all | bytes 4194304 | tf_op jit(solution)/shard_map/all_to_all | solution.py:101
  1238.8 2.9 copy.38
  1241.7 250.6 %all-gather.6.cloned.1.call-done = bf16[320,1,8192]{2,0,1:T(8,128)(2,1)} async-done(((bf16[320,1,128]{2,0,1:T(8,128)(2,1)}), bf16[320,1,8192]{2,0,1:T(8,128)(2,1)}) %all-gather.6.cloned.1.call-update) | async-done | bytes 5242896 | tf_op jit(solution)/shard_map/all_gather | solution.py:103
  1492.3 4.7 fusion.15
  1497.0 41.5 %collective-permute-start = (bf16[320,128]{1,0:T(8,128)(2,1)S(1)}, bf16[320,128]{1,0:T(8,128)(2,1)S(1)}, u32[]{:S(2)}, u32[]{:S(2)}) collective-permute-start(bf16[320,128]{1,0:T(8,128)(2,1)S(1)} %fusion.15), channel_id=1, source_target_pairs={{0,64},{64,128},{128,192},{192,256},{256,320},{320,384},{384,448},... | collective-permute-start | bytes 245768 | tf_op jit(solution)/shard_map/ppermute | solution.py:18
  1538.6 1.5 collective-permute-done
  1540.0 0.6 copy.45
  (24 shorter events, 0.1 us)
Async XLA Ops:
  6.5 881.1 %all-reduce.2.cloned.1.call-start = ((), (), s32[]{:S(2)}) async-start(), calls=%async_computation.2 | async-start | bytes 5242880 | tf_op jit(solution)/shard_map/psum | solution.py:82
  175.7 0.9 copy-start.2
  175.8 1012.4 %all-gather.4.cloned.1.call-start = ((), (), s32[]{:S(2)}) async-start(), calls=%async_computation.3 | async-start | bytes 5324800 | tf_op jit(solution)/shard_map/all_gather | solution.py:75
  177.4 3.3 copy-start.4
  177.4 3.3 copy-start.5
  182.5 741.0 %all-to-all-start = ((bf16[128,64,128]{0,2,1:T(8,128)(2,1)}), bf16[128,64,128]{0,2,1:T(8,128)(2,1)}, u32[]{:S(2)}, u32[]{:S(2)}) async-start(bf16[128,64,128]{0,2,1:T(8,128)(2,1)} %fusion.5), calls=%async_computation | async-start | bytes 4194304 | tf_op jit(solution)/shard_map/all_to_all | solution.py:77
  188.1 1304.2 %all-gather.6.cloned.1.call-start = ((), (), s32[]{:S(2)}) async-start(), calls=%async_computation.4 | async-start | bytes 5324800 | tf_op jit(solution)/shard_map/all_gather | solution.py:103
  899.0 3.7 copy-start.1
  918.0 2.7 copy-start
  932.8 261.2 %copy-start.3 = (s32[320]{0:T(512)S(1)}, s32[320]{0:T(512)}, u32[]{:S(2)}) copy-start(s32[320]{0:T(512)} %param.23) | copy-start | bytes 3844
  1197.0 3.5 copy-start.6
  1197.0 3.5 copy-start.7
  1497.0 43.0 %collective-permute-start = (bf16[320,128]{1,0:T(8,128)(2,1)S(1)}, bf16[320,128]{1,0:T(8,128)(2,1)S(1)}, u32[]{:S(2)}, u32[]{:S(2)}) collective-permute-start(bf16[320,128]{1,0:T(8,128)(2,1)S(1)} %fusion.15), channel_id=1, source_target_pairs={{0,64},{64,128},{128,192},{192,256},{256,320},{320,384},{384,448},... | collective-permute-start | bytes 245768 | tf_op jit(solution)/shard_map/ppermute | solution.py:18
Sparse Core Ops, SparseCore 0:
  175.9 711.7 all-reduce.1
  889.7 298.4 all-gather.3
  1197.1 295.1 all-gather.5
where the time goes:
time: 1550 us
  waiting for transfers between devices  1210 us (78%)
  blocking collectives  201 us (13%)
  starting transfers between devices  47.2 us (3%)
  local copies, waits for them, and re-layouts  46.4 us (3%)
  other arithmetic  16 us (1%)
  matrix products  15.9 us (1%)
    psum x1, waiting for transfers between devices, local(): lax.psum(jnp.dot(normed, kv_eff, preferred_element_type=jnp.float32), 'tp')  699 us
    all_gather x1, waiting for transfers between devices, local(): normed_all = lax.all_gather(normed, 'tp', axis=1, tiled=True)  255 us
    all_gather x1, waiting for transfers between devices, local(): lax.all_gather(head_out, 'tp', axis=1, tiled=True)  251 us
    psum x1, blocking collectives, local(): squares = lax.psum(partial_value, 'tp')  164 us
    ppermute x1, starting transfers between devices, passed_along(): return lax.ppermute(value, axis, pairs)  41.5 us
    all_to_all x1, blocking collectives, local(): lax.all_to_all(o_eff, 'tp', split_axis=1, concat_axis=0, tiled=True)  37.8 us
  transfers between devices with their start and end apart: 5, of which 4 were waited for; matrix products, arithmetic and copies ran while one was open for 4% of the time, Pallas kernels for 0%

commit v1 on v0

--- a/solution.py
+++ b/solution.py
@@ -1,7 +1,9 @@
+import functools
 import jax
 import jax.numpy as jnp
 from jax import lax
 from jax.sharding import PartitionSpec as P
+from jax.lax import all_gather
 
 D = 8192
 HEADS = 64
@@ -10,6 +12,13 @@
 BLK = 128
 rope_base = 500000.0
 epsilon = 1e-05
+
+
+def update_clusters(mine, mesh_dim):
+    return jnp.sum(all_gather(mine, mesh_dim), axis=0)
+
+
+check_sectors_on_mesh = functools.partial(update_clusters, mesh_dim="tp")
 
 
 def passed_along(value, axis, steps):
@@ -68,7 +77,7 @@
     kv_width = KV_HEADS * HD
     group_size = HEADS // KV_HEADS
     partial_value = jnp.sum(activ * activ, axis=1, keepdims=True)
-    squares = lax.psum(partial_value, "tp")
+    squares = check_sectors_on_mesh(partial_value)
     normed = (activ * lax.rsqrt(squares / D + epsilon) * norm_gain[0].astype(jnp.float32)).astype(
         jnp.bfloat16
     )

time: 1550 us -> 2000 us (1.29)
  waiting for transfers between devices: 1210 us -> 1820 us
  blocking collectives: 201 us -> 37.8 us
    unnamed x3 -> x5, waiting for transfers between devices: 0.05 us -> 624 us
    psum x1 -> x0, blocking collectives: 164 us -> none  [local(): squares = lax.psum(partial_value, 'tp')]
  transfers between devices with their start and end apart: 5 -> 6, of which waited for: 4 -> 5; matrix products, arithmetic and copies ran while one was open for 4% -> 3% of each run, Pallas kernels for 0% -> 0%
where the time goes in v1:
time: 2000 us
  waiting for transfers between devices  1820 us (91%)
  local copies, waits for them, and re-layouts  49.6 us (2%)
  starting transfers between devices  49.2 us (2%)
  blocking collectives  37.8 us (2%)
    psum x1, waiting for transfers between devices, local(): lax.psum(jnp.dot(normed, kv_eff, preferred_element_type=jnp.float32), 'tp')  687 us
    unnamed x5, waiting for transfers between devices  624 us
    all_gather x1, waiting for transfers between devices, local(): normed_all = lax.all_gather(normed, 'tp', axis=1, tiled=True)  255 us
    all_gather x1, waiting for transfers between devices, local(): lax.all_gather(head_out, 'tp', axis=1, tiled=True)  251 us
    ppermute x1, starting transfers between devices, passed_along(): return lax.ppermute(value, axis, pairs)  41.5 us
  transfers between devices with their start and end apart: 6, of which 5 were waited for; matrix products, arithmetic and copies ran while one was open for 3% of the time, Pallas kernels for 0%

profile of v1, /device:TPU:1, one launch (start us, length us, event | category | flops | bytes accessed | tf_op | source)
XLA Modules:
  0.0 2000.1 jit_solution(5034334032522002702)
XLA Ops:
  6.5 1.0 fusion.27
  7.6 1.3 dynamic-slice
  9.5 0.3 dynamic-update-slice
  9.8 0.6 copy-done.3
  10.4 0.0 all-reduce.4.cloned.1.call-start
  10.5 0.7 multiply_bitcast_fusion.2
  11.2 0.1 broadcast_bitcast_fusion
  11.2 0.7 bitcast_convert_fusion
  11.9 623.5 %all-reduce.6.cloned.1.call-done = f32[20480]{0:T(1024)} async-done(((f32[20480]{0:T(1024)}), f32[20480]{0:T(1024)}) %all-reduce.6.cloned.1.call-update) | async-done | bytes 81936
  635.4 1.0 reshape.400
  636.4 3.1 fusion.20
  639.6 0.8 copy-done.2
  640.5 0.7 fusion.29
  641.2 3.2 copy.41
  644.5 1.9 fusion.5
  646.4 7.5 all-to-all-start
  653.9 0.0 all-gather.7.cloned.1.call-start
  654.0 686.6 %all-reduce.4.cloned.1.call-done = f32[320,2048]{1,0:T(8,128)} async-done(((f32[320,2048]{1,0:T(8,128)}), f32[320,2048]{1,0:T(8,128)}) %all-reduce.4.cloned.1.call-update) | async-done | bytes 2621456 | tf_op jit(solution)/shard_map/psum | solution.py:91
  1340.7 3.5 copy.36
  1344.1 3.7 reshape.392
  1347.9 4.1 fusion.55
  1352.0 3.7 copy.48
  1355.7 3.4 copy.49
  1359.1 7.1 multiply_subtract_fusion
  1366.2 0.1 pad_maximum_fusion
  1366.3 2.4 copy.39
  1368.7 2.2 reshape.393
  1370.9 2.7 copy.40
  1373.6 2.8 select_convert_fusion
  1376.5 3.2 copy.42
  1379.7 3.0 copy.43
  1382.7 3.2 dot_general.21
  1385.9 255.4 %all-gather.5.cloned.1.call-done = bf16[320,8192]{1,0:T(8,128)(2,1)} async-done(((bf16[320,128]{1,0:T(8,128)(2,1)}), bf16[320,8192]{1,0:T(8,128)(2,1)}) %all-gather.5.cloned.1.call-update) | async-done | bytes 5242896 | tf_op jit(solution)/shard_map/all_gather | solution.py:84
  1641.2 5.1 fusion.2
  1646.3 0.5 subtract_convert_fusion
  1646.8 0.1 copy.45
  1646.9 0.1 convert_element_type.151
  1647.0 1.2 fusion.56
  1648.2 1.8 fusion.18
  1650.0 3.4 copy.46
  1653.5 0.5 fusion.4
  1654.0 37.8 %all_to_all.32 = bf16[128,64,128]{0,2,1:T(8,128)(2,1)S(1)} all-to-all(bf16[128,64,128]{0,2,1:T(8,128)(2,1)S(1)} %fusion.4), channel_id=1, replica_groups=mesh['section'=8,'tp'=64] {'tp'}, dimensions={1} | all-to-all | bytes 4194304 | tf_op jit(solution)/shard_map/all_to_all | solution.py:110
  1691.8 2.9 copy.47
  1694.7 250.5 %all-gather.7.cloned.1.call-done = bf16[320,1,8192]{2,0,1:T(8,128)(2,1)} async-done(((bf16[320,1,128]{2,0,1:T(8,128)(2,1)}), bf16[320,1,8192]{2,0,1:T(8,128)(2,1)}) %all-gather.7.cloned.1.call-update) | async-done | bytes 5242896 | tf_op jit(solution)/shard_map/all_gather | solution.py:112
  1945.2 4.7 fusion.15
  1949.9 41.5 %collective-permute-start = (bf16[320,128]{1,0:T(8,128)(2,1)S(1)}, bf16[320,128]{1,0:T(8,128)(2,1)S(1)}, u32[]{:S(2)}, u32[]{:S(2)}) collective-permute-start(bf16[320,128]{1,0:T(8,128)(2,1)S(1)} %fusion.15), channel_id=1, source_target_pairs={{0,64},{64,128},{128,192},{192,256},{256,320},{320,384},{384,448},... | collective-permute-start | bytes 245768 | tf_op jit(solution)/shard_map/ppermute | solution.py:27
  1991.5 1.5 collective-permute-done
  1992.9 0.6 copy.56
  (32 shorter events, 0.3 us)
Async XLA Ops:
  6.5 628.9 %all-reduce.6.cloned.1.call-start = ((), (), s32[]{:S(2)}) async-start(), calls=%async_computation.5 | async-start | bytes 163840
  9.8 0.6 copy-start.3
  10.4 1330.2 %all-reduce.4.cloned.1.call-start = ((), (), s32[]{:S(2)}) async-start(), calls=%async_computation.2 | async-start | bytes 5242880 | tf_op jit(solution)/shard_map/psum | solution.py:91
  639.6 0.9 copy-start.2
  639.6 1001.6 %all-gather.5.cloned.1.call-start = ((), (), s32[]{:S(2)}) async-start(), calls=%async_computation.3 | async-start | bytes 5324800 | tf_op jit(solution)/shard_map/all_gather | solution.py:84
  641.2 3.3 copy-start.5
  641.2 3.3 copy-start.6
  646.4 730.1 %all-to-all-start = ((bf16[128,64,128]{0,2,1:T(8,128)(2,1)}), bf16[128,64,128]{0,2,1:T(8,128)(2,1)}, u32[]{:S(2)}, u32[]{:S(2)}) async-start(bf16[128,64,128]{0,2,1:T(8,128)(2,1)} %fusion.5), calls=%async_computation | async-start | bytes 4194304 | tf_op jit(solution)/shard_map/all_to_all | solution.py:86
  653.9 1291.3 %all-gather.7.cloned.1.call-start = ((), (), s32[]{:S(2)}) async-start(), calls=%async_computation.4 | async-start | bytes 5324800 | tf_op jit(solution)/shard_map/all_gather | solution.py:112
  1352.0 3.7 copy-start.1
  1370.9 2.7 copy-start
  1385.8 261.2 %copy-start.4 = (s32[320]{0:T(512)S(1)}, s32[320]{0:T(512)}, u32[]{:S(2)}) copy-start(s32[320]{0:T(512)} %param.23) | copy-start | bytes 3844
  1650.0 3.5 copy-start.7
  1650.0 3.5 copy-start.8
  1949.9 43.0 %collective-permute-start = (bf16[320,128]{1,0:T(8,128)(2,1)S(1)}, bf16[320,128]{1,0:T(8,128)(2,1)S(1)}, u32[]{:S(2)}, u32[]{:S(2)}) collective-permute-start(bf16[320,128]{1,0:T(8,128)(2,1)S(1)} %fusion.15), channel_id=1, source_target_pairs={{0,64},{64,128},{128,192},{192,256},{256,320},{320,384},{384,448},... | collective-permute-start | bytes 245768 | tf_op jit(solution)/shard_map/ppermute | solution.py:27
Sparse Core Ops, SparseCore 0:
  10.6 624.7 all-reduce.5
  639.7 700.9 all-reduce.3
  1342.7 298.4 all-gather.4
  1650.1 295.0 all-gather.6
